TPU v7x, 32 devices: a whole 2x2x4 slice. The times are simulated.
32 devices in a mesh: sub: 8 (over y, x, core), grp: 4 (over z).
Axes of the slice: x: 2, y: 2, z: 4, core: 2. Of those that a mesh axis runs over, the one named last changes fastest.
Arguments:
- gaps: float32 [4, 16, 96, 1024], P('grp', 'sub'), may hold values from -6 to 6
- dual_op: bfloat16 [4, 16, 1024, 1024], P('grp', 'sub'), may hold values from -1 to 2.5, as said below
- dirichlet: bfloat16 [4, 16, 1024, 1024], P('grp', 'sub'), may hold values from -1 to 2.5, as said below
- modes: float32 [4, 16, 6, 1024], P('grp', 'sub'), may hold values from -6 to 6
- coarse_op: float32 [4, 16, 6, 384], P('grp', 'sub'), may hold values from -0.0009765625 to 0.0009765625, as said below
- slot_map: int32 [4, 16, 1024], P('grp', 'sub'), may hold values from 0 to 1023, as said below
Outputs:
- multipliers: float32 [4, 16, 96, 1024], P('grp', 'sub')
- residual: float32 [4, 16, 96, 1024], P('grp', 'sub')
Inputs may be any that keep to these rules, and one draw needn't show every extreme that they name: `dual_op`: each subdomain's block is symmetric positive definite. `dirichlet`: each subdomain's block is symmetric positive definite. The 384 x 384 matrix whose row (16 y + x) * 6 + k is coarse_op[y, x, k] is symmetric. `slot_map`: for every subdomain and face f, the entries f * 256 to (f + 1) * 256 - 1 are a permutation of those same slot numbers.
All inputs are finite; a program needn't handle non-finite values.
Results may differ from a plain program's by a relative error of at most 0.012.
The roundings to bfloat16 on the way count: a program that leaves them out, or rounds other values in their place, can miss the bound.
Values sent between devices are 32-bit elements; how exact they have to be, the bound alone decides.
No kernel may reach another device: no remote copies, remote signals or barrier semaphores. Data moves between devices by JAX's collectives and lax.ppermute only.
A program may use at most 128 MiB of HBM per device.

v0:
```python
import jax
import jax.numpy as jnp
from jax import lax
from jax.sharding import PartitionSpec as P

MODES = 6
ITERS = 2
HIGHEST = lax.Precision.HIGHEST


def extended(block, sides, width):
    for axis, dim in sides:
        count = lax.axis_size(axis)
        forward = [(i, i + 1) for i in range(count - 1)]
        backward = [(target, source) for source, target in forward]
        low = lax.ppermute(
            lax.slice_in_dim(block, block.shape[dim] - width, None, axis=dim), axis, forward
        )
        high = lax.ppermute(lax.slice_in_dim(block, 0, width, axis=dim), axis, backward)
        block = jnp.concatenate([low, block, high], axis=dim)
    return block


def inverse_map(maps):
    width = maps.shape[-1]

    def invert(perm_row):
        return jnp.zeros_like(perm_row).at[perm_row].set(jnp.arange(width, dtype=jnp.int32))

    return jax.vmap(invert)(maps)


def reorder_block(matrix, order):
    rows_first = jnp.take(matrix, order, axis=0)
    swapped = jnp.swapaxes(rows_first, 0, 1)
    both = jnp.take(swapped, order, axis=0)
    return jnp.swapaxes(both, 0, 1)


def jump_local(values):
    subdomains, columns, width = values.shape
    faces = values.reshape(subdomains, columns, 4, width // 4)
    edges = jnp.stack([faces[0, :, 0], faces[-1, :, 1]])
    beside = extended(edges, (("sub", 0),), 1)
    rims = jnp.stack([faces[:, :, 2], faces[:, :, 3]])
    across = extended(rims, (("grp", 0),), 1)
    from_left = jnp.concatenate([beside[0][None], faces[:-1, :, 1]], axis=0)
    from_right = jnp.concatenate([faces[1:, :, 0], beside[3][None]], axis=0)
    partner = jnp.stack([from_left, from_right, across[0], across[3]], axis=2)
    return (faces - partner).reshape(subdomains, columns, width)


def apply_blocks(values, matrices):
    return jnp.einsum(
        "snm,smk->snk", values.astype(jnp.bfloat16), matrices, preferred_element_type=jnp.float32
    )


def shards(gaps, dual_op, dirichlet, modes, coarse_op, slot_map):
    maps = slot_map[0]
    back_map = inverse_map(maps)
    vectors = jnp.take_along_axis(gaps[0], maps[:, None, :], axis=2)
    subdomains, columns, width = vectors.shape
    quarter = width // 4
    sub_total = lax.axis_size("sub")
    grp_total = lax.axis_size("grp")
    x_position = lax.axis_index("sub") * subdomains + jnp.arange(subdomains, dtype=jnp.int32)
    grp_here = lax.axis_index("grp")
    filler = jnp.ones((subdomains,), jnp.float32)
    face_weight = jnp.stack(
        [
            jnp.where(x_position == 0, 1.0, 2.0) * filler,
            jnp.where(x_position == sub_total * subdomains - 1, 1.0, 2.0) * filler,
            jnp.where(grp_here == 0, 1.0, 2.0) * filler,
            jnp.where(grp_here == grp_total - 1, 1.0, 2.0) * filler,
        ],
        axis=1,
    )
    slot_weight = jnp.repeat(face_weight, quarter, axis=1)
    ordered_modes = jnp.take_along_axis(modes[0], maps[:, None, :], axis=2)
    weighted_modes = ordered_modes * slot_weight[:, None, :]
    stiffness = jax.vmap(reorder_block)(dual_op[0], maps)
    schur_blocks = jax.vmap(reorder_block)(dirichlet[0], maps)
    rows_here = coarse_op[0].reshape(subdomains * MODES, -1)
    rows_count = rows_here.shape[0]
    rows_sub_major = rows_here.reshape(rows_count, grp_total, sub_total, rows_count)
    rows_sub_major = rows_sub_major.transpose(0, 2, 1, 3).reshape(rows_count, -1)
    coarse_total = rows_here.shape[1]
    face_modes = ordered_modes.reshape(subdomains, MODES, 4, quarter).transpose(0, 2, 1, 3)
    own_rows = rows_here.reshape(subdomains, 1, MODES, coarse_total)
    packed = jnp.concatenate(
        [face_modes, jnp.broadcast_to(own_rows, (subdomains, 4, MODES, coarse_total))], axis=3
    )
    edge_pack = jnp.stack([packed[0, 0], packed[-1, 1]])
    beside_pack = extended(edge_pack, (("sub", 0),), 1)
    rim_pack = jnp.stack([packed[:, 2], packed[:, 3]])
    across_pack = extended(rim_pack, (("grp", 0),), 1)
    left_pack = jnp.concatenate([beside_pack[0][None], packed[:-1, 1]], axis=0)
    right_pack = jnp.concatenate([packed[1:, 0], beside_pack[3][None]], axis=0)
    partner_pack = jnp.stack([left_pack, right_pack, across_pack[0], across_pack[3]], axis=1)
    partner_modes = partner_pack[:, :, :, :quarter]
    partner_rows = partner_pack[:, :, :, quarter:]

    def coefficients(values):
        return jnp.einsum("skm,snm->skn", weighted_modes, values, precision=HIGHEST)

    def gathered(coeffs):
        grouped = lax.all_gather(coeffs[None], "grp", axis=0, tiled=True)
        everything = lax.all_gather(grouped, "sub", axis=1, tiled=True)
        return everything.reshape(-1, columns)

    def amounts_of(flat):
        return jnp.dot(rows_here, flat, precision=HIGHEST, preferred_element_type=jnp.float32)

    def lift(amounts, flat):
        shaped = amounts.reshape(subdomains, MODES, columns)
        own_face = jnp.einsum("sfkm,skn->snfm", face_modes, shaped, precision=HIGHEST)
        far_amounts = jnp.einsum("sfkc,cn->sfkn", partner_rows, flat, precision=HIGHEST)
        far_face = jnp.einsum("sfkm,sfkn->snfm", partner_modes, far_amounts, precision=HIGHEST)
        return (own_face - far_face).reshape(subdomains, columns, width)

    def project(values):
        flat = gathered(coefficients(values))
        return values - lift(amounts_of(flat), flat)

    dual = jump_local(vectors)
    multipliers = jnp.zeros_like(dual)
    residual = project(dual)
    direction = jnp.zeros_like(dual)
    rho_prev = jnp.ones((columns,), jnp.float32)
    for step_index in range(ITERS):
        projected = project(residual)
        precond = jump_local(apply_blocks(projected, schur_blocks))
        rho_now = lax.psum(jnp.sum(projected * precond, axis=(0, 2)), ("sub", "grp"))
        search = project(precond)
        if step_index > 0:
            search = search + (rho_now / rho_prev)[None, :, None] * direction
        direction = search
        image = jump_local(apply_blocks(direction, stiffness))
        partial_dot = jnp.sum(direction * image, axis=(0, 2))
        curvature = lax.psum(partial_dot, ("sub", "grp"))
        step_len = rho_now / curvature
        multipliers = multipliers + step_len[None, :, None] * direction
        residual = residual - step_len[None, :, None] * image
        rho_prev = rho_now
    multipliers = jnp.take_along_axis(multipliers, back_map[:, None, :], axis=2)
    residual = jnp.take_along_axis(residual, back_map[:, None, :], axis=2)
    return (multipliers[None], residual[None])


def solution(mesh):
    placed = (
        P("grp", "sub", None, None),
        P("grp", "sub", None, None),
        P("grp", "sub", None, None),
        P("grp", "sub", None, None),
        P("grp", "sub", None, None),
        P("grp", "sub", None),
    )
    return jax.shard_map(
        shards,
        mesh=mesh,
        in_specs=placed,
        out_specs=(P("grp", "sub", None, None), P("grp", "sub", None, None)),
        check_vma=False,
    )
```

profile of v0, /device:TPU:0, one launch (start us, length us, event | category | flops | bytes accessed | tf_op | source)
XLA Modules:
  0.0 632.0 jit_solution(5257530324860456469)
XLA Ops:
  2.6 13.0 %gather_fusion = f32[2048,6]{1,0:T(8,128)S(1)} fusion(f32[2,6,1024]{1,2,0:T(8,128)S(1)} %bitcast.393, s32[2048]{0:T(1024)S(1)} %get-tuple-element.61), kind=kCustom, calls=%fused_computation.7 | custom fusion | bytes 114688 | tf_op jit(solution)/shard_map/jit(take_along_axis)/gather | solution.py:80
  17.6 2.4 collective-permute-start.4
  19.9 1.3 collective-permute-start.5
  21.3 4.3 collective-permute-start.6
  25.6 1.3 collective-permute-start.7
  27.3 13.0 %gather_fusion.1 = f32[2048,96]{1,0:T(8,128)S(1)} fusion(f32[2,96,1024]{1,2,0:T(8,128)S(1)} %bitcast.378, s32[2048]{0:T(1024)S(1)} %bitcast.377), kind=kCustom, calls=%fused_computation.clone | custom fusion | bytes 1589248 | tf_op jit(solution)/shard_map/jit(take_along_axis)/gather | solution.py:62
  41.5 4.0 collective-permute-start
  46.2 42.2 %gather_fusion.2 = bf16[2048,1024]{1,0:T(8,128)(2,1)} fusion(bf16[2,1024,1024]{2,1,0:T(8,128)(2,1)} %bitcast.375, s32[2048]{0:T(1024)S(1)} %get-tuple-element.60), kind=kCustom, calls=%fused_computation.1.clone | custom fusion | bytes 8404992 | tf_op jit(solution)/shard_map/vmap(jit(_take))/gather | solution.py:34
  88.4 6.2 copy.139
  94.6 42.0 %gather_fusion.4 = bf16[2048,1024]{1,0:T(8,128)(2,1)} fusion(bf16[2,1024,1024]{2,1,0:T(8,128)(2,1)} %bitcast.376, s32[2048]{0:T(1024)S(1)} %get-tuple-element.60), kind=kCustom, calls=%fused_computation.5.clone | custom fusion | bytes 8404992 | tf_op jit(solution)/shard_map/vmap(jit(_take))/gather | solution.py:34
  136.6 6.3 copy.148
  143.1 8.0 %scatter_custom_fusion = s32[2048]{0:T(1024)S(1)} fusion(s32[2048]{0:T(1024)S(1)} %get-tuple-element.65, s32[2048]{0:T(1024)S(1)} %get-tuple-element.64, s32[]{:T(128)} %constant.29.clone.1), kind=kCustom, calls=%fused_computation.184 | custom fusion | bytes 8196
  151.3 7.5 %select_bitcast_fusion = (bf16[2,1024,1024]{2,1,0:T(8,128)(2,1)}, bf16[2,1024,1024]{2,1,0:T(8,128)(2,1)}) fusion(bf16[2,1024,1024]{1,2,0:T(8,128)(2,1)} %copy.148, pred[2,1024]{1,0:T(4,128)(4,1)S(1)} %compare_and_fusion.1, bf16[2,1024,1024]{1,2,0:T(8,128)(2,1)} %copy.139), kind=kLoop, calls=%fused_computation.9 | loop fusion | flops 4194304 | bytes 16779264 | tf_op jit(solution)/shard_map/vmap()/transpose | solution.py:35
  159.4 40.6 %gather_fusion.3 = bf16[2048,1024]{1,0:T(8,128)(2,1)} fusion(bf16[2,1024,1024]{2,1,0:T(8,128)(2,1)} %get-tuple-element.57, s32[2048]{0:T(1024)S(1)} %get-tuple-element.60), kind=kCustom, calls=%fused_computation.4.clone | custom fusion | bytes 8404992 | tf_op jit(solution)/shard_map/vmap(jit(_take))/gather | solution.py:36
  200.0 40.7 %gather_fusion.5 = bf16[2048,1024]{1,0:T(8,128)(2,1)} fusion(bf16[2,1024,1024]{2,1,0:T(8,128)(2,1)} %get-tuple-element.56, s32[2048]{0:T(1024)S(1)} %get-tuple-element.60), kind=kCustom, calls=%fused_computation.6.clone | custom fusion | bytes 8404992 | tf_op jit(solution)/shard_map/vmap(jit(_take))/gather | solution.py:36
  242.0 4.1 collective-permute-start.2
  246.2 1.5 collective-permute-start.3
  249.3 4.6 collective-permute-done.3
  255.9 13.5 %all-gather = f32[8,6,96]{2,1,0:T(8,128)S(1)} all-gather(f32[2,6,96]{2,1,0:T(8,128)S(1)} %fusion.40), channel_id=2, replica_groups=mesh['sub'=8,'grp'=4] {'grp'}, dimensions={0}, use_global_device_ids=true | all-gather | bytes 23040 | tf_op jit(solution)/shard_map/all_gather | solution.py:108
  269.5 13.7 %all_gather.31 = f32[4,16,6,96]{3,2,1,0:T(8,128)S(1)} all-gather(f32[4,2,6,96]{3,2,1,0:T(8,128)S(1)} %bitcast.410), channel_id=1, replica_groups=mesh['sub'=8,'grp'=4] {'sub'}, dimensions={1}, use_global_device_ids=true | all-gather | bytes 165888 | tf_op jit(solution)/shard_map/all_gather | solution.py:109
  286.4 13.1 %all-gather.1 = f32[8,6,96]{2,1,0:T(8,128)S(1)} all-gather(f32[2,6,96]{2,1,0:T(8,128)S(1)} %fusion.38), channel_id=3, replica_groups=mesh['sub'=8,'grp'=4] {'grp'}, dimensions={0}, use_global_device_ids=true | all-gather | bytes 23040 | tf_op jit(solution)/shard_map/all_gather | solution.py:108
  299.5 7.9 %all_gather.33 = f32[4,16,6,96]{3,2,1,0:T(8,128)S(1)} all-gather(f32[4,2,6,96]{3,2,1,0:T(8,128)S(1)} %bitcast.411), channel_id=1, replica_groups=mesh['sub'=8,'grp'=4] {'sub'}, dimensions={1}, use_global_device_ids=true | all-gather | bytes 165888 | tf_op jit(solution)/shard_map/all_gather | solution.py:109
  310.2 1.7 fusion.1
  312.6 2.3 collective-permute-start.8
  315.2 1.3 collective-permute-start.9
  316.5 1.5 collective-permute-start.10
  318.1 1.5 collective-permute-start.11
  320.4 1.4 collective-permute-done.10
  321.8 4.7 collective-permute-done.11
  327.7 1.4 multiply_reduce_fusion.3
  329.9 13.2 %all-gather.2 = f32[8,6,96]{2,1,0:T(8,128)S(1)} all-gather(f32[2,6,96]{2,1,0:T(8,128)S(1)} %fusion.36), channel_id=4, replica_groups=mesh['sub'=8,'grp'=4] {'grp'}, dimensions={0}, use_global_device_ids=true | all-gather | bytes 23040 | tf_op jit(solution)/shard_map/all_gather | solution.py:108
  343.0 11.7 %all_gather.35 = f32[4,16,6,96]{3,2,1,0:T(8,128)S(1)} all-gather(f32[4,2,6,96]{3,2,1,0:T(8,128)S(1)} %bitcast.412), channel_id=1, replica_groups=mesh['sub'=8,'grp'=4] {'sub'}, dimensions={1}, use_global_device_ids=true | all-gather | bytes 165888 | tf_op jit(solution)/shard_map/all_gather | solution.py:109
  357.5 1.8 fusion.3
  360.0 2.3 collective-permute-start.12
  362.6 1.3 collective-permute-start.13
  363.9 1.6 collective-permute-start.14
  367.6 3.0 collective-permute-done.14
  370.6 4.4 collective-permute-done.15
  377.1 1.7 multiply_reduce_fusion.2
  378.7 39.3 %all-reduce = (f32[96]{0:T(128)S(1)}, f32[96]{0:T(128)S(1)}) all-reduce(f32[96]{0:T(128)S(1)} %get-tuple-element.12, f32[96]{0:T(128)S(1)} %get-tuple-element.10), channel_id=1, replica_groups=mesh['sub'=8,'grp'=4] {'sub','grp'}, use_global_device_ids=true, to_apply=%region_1.4 | all-reduce | flops 192 | bytes 1536 | tf_op jit(solution)/shard_map/psum | solution.py:134
  419.0 13.1 %all-gather.3 = f32[8,6,96]{2,1,0:T(8,128)S(1)} all-gather(f32[2,6,96]{2,1,0:T(8,128)S(1)} %fusion.34), channel_id=5, replica_groups=mesh['sub'=8,'grp'=4] {'grp'}, dimensions={0}, use_global_device_ids=true | all-gather | bytes 23040 | tf_op jit(solution)/shard_map/all_gather | solution.py:108
  432.1 10.5 %all_gather.37 = f32[4,16,6,96]{3,2,1,0:T(8,128)S(1)} all-gather(f32[4,2,6,96]{3,2,1,0:T(8,128)S(1)} %bitcast.413), channel_id=1, replica_groups=mesh['sub'=8,'grp'=4] {'sub'}, dimensions={1}, use_global_device_ids=true | all-gather | bytes 165888 | tf_op jit(solution)/shard_map/all_gather | solution.py:109
  445.9 1.8 fusion
  448.4 2.3 collective-permute-start.16
  453.6 4.6 collective-permute-start.18
  459.0 2.3 collective-permute-done.19
  461.3 1.8 collective-permute-done.18
  463.8 1.3 stack.96
  465.1 1.9 multiply_reduce_fusion.1
  467.7 13.2 %all-gather.4 = f32[8,6,96]{2,1,0:T(8,128)S(1)} all-gather(f32[2,6,96]{2,1,0:T(8,128)S(1)} %fusion.32), channel_id=6, replica_groups=mesh['sub'=8,'grp'=4] {'grp'}, dimensions={0}, use_global_device_ids=true | all-gather | bytes 23040 | tf_op jit(solution)/shard_map/all_gather | solution.py:108
  480.9 10.2 %all_gather.39 = f32[4,16,6,96]{3,2,1,0:T(8,128)S(1)} all-gather(f32[4,2,6,96]{3,2,1,0:T(8,128)S(1)} %bitcast.414), channel_id=1, replica_groups=mesh['sub'=8,'grp'=4] {'sub'}, dimensions={1}, use_global_device_ids=true | all-gather | bytes 165888 | tf_op jit(solution)/shard_map/all_gather | solution.py:109
  491.7 38.7 %psum.30 = f32[96]{0:T(128)S(1)} all-reduce(f32[96]{0:T(128)S(1)} %get-tuple-element.8), channel_id=1, replica_groups=mesh['sub'=8,'grp'=4] {'sub','grp'}, use_global_device_ids=true, to_apply=%region_5.8 | all-reduce | flops 96 | bytes 768 | tf_op jit(solution)/shard_map/psum | solution.py:134
  532.6 2.5 fusion.2
  535.1 1.5 reshape.211
  536.9 1.3 collective-permute-start.20
  539.8 3.4 collective-permute-start.22
  546.4 4.4 collective-permute-done.23
  552.8 2.5 multiply_reduce_fusion
  555.4 43.3 %psum.31 = f32[96]{0:T(128)S(1)} all-reduce(f32[96]{0:T(128)S(1)} %get-tuple-element.6), channel_id=1, replica_groups=mesh['sub'=8,'grp'=4] {'sub','grp'}, use_global_device_ids=true, to_apply=%region_7.10 | all-reduce | flops 96 | bytes 768 | tf_op jit(solution)/shard_map/psum | solution.py:141
  598.7 2.3 multiply_subtract_fusion
  601.0 1.5 copy.169
  602.5 13.0 %gather_fusion.6 = f32[2048,96]{1,0:T(8,128)S(1)} fusion(f32[2,96,1024]{1,2,0:T(8,128)S(1)} %copy.169, s32[2048]{0:T(1024)S(1)} %bitcast.373), kind=kCustom, calls=%fused_computation.2.clone | custom fusion | bytes 1589248 | tf_op jit(solution)/shard_map/jit(take_along_axis)/gather | solution.py:146
  617.1 13.0 %gather_fusion.7 = f32[2048,96]{1,0:T(8,128)S(1)} fusion(f32[2,96,1024]{1,2,0:T(8,128)S(1)} %copy.171, s32[2048]{0:T(1024)S(1)} %bitcast.374), kind=kCustom, calls=%fused_computation.3.clone | custom fusion | bytes 1589248 | tf_op jit(solution)/shard_map/jit(take_along_axis)/gather | solution.py:147
  630.5 1.3 select_bitcast_fusion.2
  (192 shorter events, 50.8 us)
Async XLA Ops:
  0.6 26.3 %copy-start.10 = (s32[1,2,1024]{2,1,0:T(2,128)S(1)}, s32[1,2,1024]{2,1,0:T(2,128)}, u32[]{:S(2)}) copy-start(s32[1,2,1024]{2,1,0:T(2,128)} %param.15) | copy-start | bytes 24580
  0.6 26.3 %copy-start.9 = (f32[1,2,96,1024]{3,2,1,0:T(8,128)S(1)}, f32[1,2,96,1024]{3,2,1,0:T(8,128)}, u32[]{:S(2)}) copy-start(f32[1,2,96,1024]{3,2,1,0:T(8,128)} %param.10) | copy-start | bytes 2359300
  17.6 223.1 %collective-permute-start.4 = (f32[1,6,640]{2,1,0:T(8,128)S(1)}, f32[1,6,640]{2,1,0:T(8,128)S(1)}, u32[]{:S(2)}, u32[]{:S(2)}) collective-permute-start(f32[1,6,640]{2,1,0:T(8,128)S(1)} %get-tuple-element.44), channel_id=1, source_target_pairs={{0,4},{4,8},{8,12},{12,16},{16,20},{20,24},{24,28},{1,5},{5,9},{9,... | collective-permute-start | bytes 46088 | tf_op jit(solution)/shard_map/ppermute | solution.py:16
  19.9 222.1 %collective-permute-start.5 = (f32[1,6,640]{2,1,0:T(8,128)S(1)}, f32[1,6,640]{2,1,0:T(8,128)S(1)}, u32[]{:S(2)}, u32[]{:S(2)}) collective-permute-start(f32[1,6,640]{2,1,0:T(8,128)S(1)} %get-tuple-element.45), channel_id=1, source_target_pairs={{4,0},{8,4},{12,8},{16,12},{20,16},{24,20},{28,24},{5,1},{9,5},{13... | collective-permute-start | bytes 46088 | tf_op jit(solution)/shard_map/ppermute | solution.py:19
  21.3 224.9 %collective-permute-start.6 = (f32[1,2,6,640]{3,2,1,0:T(8,128)S(1)}, f32[1,2,6,640]{3,2,1,0:T(8,128)S(1)}, u32[]{:S(2)}, u32[]{:S(2)}) collective-permute-start(f32[1,2,6,640]{3,2,1,0:T(8,128)S(1)} %get-tuple-element.48), channel_id=1, source_target_pairs={{0,1},{1,2},{2,3},{4,5},{5,6},{6,7},{8,9},{9,10},{10,11},{12,13},{... | collective-permute-start | bytes 92168 | tf_op jit(solution)/shard_map/ppermute | solution.py:16
  25.6 222.0 %collective-permute-start.7 = (f32[1,2,6,640]{3,2,1,0:T(8,128)S(1)}, f32[1,2,6,640]{3,2,1,0:T(8,128)S(1)}, u32[]{:S(2)}, u32[]{:S(2)}) collective-permute-start(f32[1,2,6,640]{3,2,1,0:T(8,128)S(1)} %get-tuple-element.49), channel_id=1, source_target_pairs={{1,0},{2,1},{3,2},{5,4},{6,5},{7,6},{9,8},{10,9},{11,10},{13,12},{... | collective-permute-start | bytes 92168 | tf_op jit(solution)/shard_map/ppermute | solution.py:19
  41.5 206.2 %collective-permute-start = (f32[1,96,256]{2,0,1:T(1,128)S(1)}, f32[1,96,256]{2,0,1:T(1,128)S(1)}, u32[]{:S(2)}, u32[]{:S(2)}) collective-permute-start(f32[1,96,256]{2,0,1:T(1,128)S(1)} %get-tuple-element.38), channel_id=1, source_target_pairs={{0,4},{4,8},{8,12},{12,16},{16,20},{20,24},{24,28},{1,5},{5,9},{9,... | collective-permute-start | bytes 294920 | tf_op jit(solution)/shard_map/ppermute | solution.py:16
  45.9 105.4 %copy-start.12 = (pred[2,1024]{1,0:T(4,128)(4,1)}, pred[2,1024]{1,0:T(4,128)(4,1)S(1)}, u32[]{:S(2)}) copy-start(pred[2,1024]{1,0:T(4,128)(4,1)S(1)} %compare_and_fusion.1) | copy-start | bytes 6148
  136.6 6.3 copy-start.15
  136.6 6.4 %copy-start.16 = (s32[2]{0:T(128)S(1)}, s32[2]{0:T(128)}, u32[]{:S(2)}) copy-start(s32[2]{0:T(128)} %constant.70) | copy-start | bytes 28
  151.3 8.1 %copy-start.11 = (f32[1,2,6,384]{3,1,2,0:T(2,128)S(1)}, f32[1,2,6,384]{3,1,2,0:T(2,128)}, u32[]{:S(2)}) copy-start(f32[1,2,6,384]{3,1,2,0:T(2,128)} %param.14) | copy-start | bytes 55300
  240.7 7.4 %collective-permute-start.1 = (f32[1,96,256]{2,0,1:T(1,128)S(1)}, f32[1,96,256]{2,0,1:T(1,128)S(1)}, u32[]{:S(2)}, u32[]{:S(2)}) collective-permute-start(f32[1,96,256]{2,0,1:T(1,128)S(1)} %get-tuple-element.39), channel_id=1, source_target_pairs={{4,0},{8,4},{12,8},{16,12},{20,16},{24,20},{28,24},{5,1},{9,5},{13... | collective-permute-start | bytes 294920 | tf_op jit(solution)/shard_map/ppermute | solution.py:19
  242.0 7.3 %collective-permute-start.2 = (f32[1,2,96,256]{3,0,2,1:T(1,128)S(1)}, f32[1,2,96,256]{3,0,2,1:T(1,128)S(1)}, u32[]{:S(2)}, u32[]{:S(2)}) collective-permute-start(f32[1,2,96,256]{3,0,2,1:T(1,128)S(1)} %get-tuple-element.42), channel_id=1, source_target_pairs={{0,1},{1,2},{2,3},{4,5},{5,6},{6,7},{8,9},{9,10},{10,11},{12,13},{... | collective-permute-start | bytes 589832 | tf_op jit(solution)/shard_map/ppermute | solution.py:16
  246.2 7.7 %collective-permute-start.3 = (f32[1,2,96,256]{3,0,2,1:T(1,128)S(1)}, f32[1,2,96,256]{3,0,2,1:T(1,128)S(1)}, u32[]{:S(2)}, u32[]{:S(2)}) collective-permute-start(f32[1,2,96,256]{3,0,2,1:T(1,128)S(1)} %get-tuple-element.43), channel_id=1, source_target_pairs={{1,0},{2,1},{3,2},{5,4},{6,5},{7,6},{9,8},{10,9},{11,10},{13,12},{... | collective-permute-start | bytes 589832 | tf_op jit(solution)/shard_map/ppermute | solution.py:19
  285.6 24.2 %copy-start.13 = (pred[2,1024]{1,0:T(4,128)(4,1)S(1)}, pred[2,1024]{1,0:T(4,128)(4,1)}, u32[]{:S(2)}) copy-start(pred[2,1024]{1,0:T(4,128)(4,1)} %copy-done.12) | copy-start | bytes 6148
  308.0 2.2 copy-start.2
  309.9 2.4 copy-start.8
  312.6 7.0 %collective-permute-start.8 = (f32[1,96,256]{2,0,1:T(1,128)S(1)}, f32[1,96,256]{2,0,1:T(1,128)S(1)}, u32[]{:S(2)}, u32[]{:S(2)}) collective-permute-start(f32[1,96,256]{2,0,1:T(1,128)S(1)} %get-tuple-element.32), channel_id=1, source_target_pairs={{0,4},{4,8},{8,12},{12,16},{16,20},{20,24},{24,28},{1,5},{5,9},{9,... | collective-permute-start | bytes 294920 | tf_op jit(solution)/shard_map/ppermute | solution.py:16
  315.2 4.8 collective-permute-start.9
  316.5 5.3 collective-permute-start.10
  318.1 8.5 %collective-permute-start.11 = (f32[1,2,96,256]{3,0,2,1:T(1,128)S(1)}, f32[1,2,96,256]{3,0,2,1:T(1,128)S(1)}, u32[]{:S(2)}, u32[]{:S(2)}) collective-permute-start(f32[1,2,96,256]{3,0,2,1:T(1,128)S(1)} %get-tuple-element.37), channel_id=1, source_target_pairs={{1,0},{2,1},{3,2},{5,4},{6,5},{7,6},{9,8},{10,9},{11,10},{13,12},{... | collective-permute-start | bytes 589832 | tf_op jit(solution)/shard_map/ppermute | solution.py:19
  355.3 2.2 copy-start
  359.3 16.5 %copy-start.6 = (f32[2,96,1024]{2,1,0:T(8,128)}, f32[2,96,1024]{2,1,0:T(8,128)S(1)}, u32[]{:S(2)}) copy-start(f32[2,96,1024]{2,1,0:T(8,128)S(1)} %fusion.3) | copy-start | bytes 2359300
  360.0 6.9 %collective-permute-start.12 = (f32[1,96,256]{2,0,1:T(1,128)S(1)}, f32[1,96,256]{2,0,1:T(1,128)S(1)}, u32[]{:S(2)}, u32[]{:S(2)}) collective-permute-start(f32[1,96,256]{2,0,1:T(1,128)S(1)} %get-tuple-element.26), channel_id=1, source_target_pairs={{0,4},{4,8},{8,12},{12,16},{16,20},{20,24},{24,28},{1,5},{5,9},{9,... | collective-permute-start | bytes 294920 | tf_op jit(solution)/shard_map/ppermute | solution.py:16
  362.6 4.7 collective-permute-start.13
  363.9 6.7 %collective-permute-start.14 = (f32[1,2,96,256]{3,0,2,1:T(1,128)S(1)}, f32[1,2,96,256]{3,0,2,1:T(1,128)S(1)}, u32[]{:S(2)}, u32[]{:S(2)}) collective-permute-start(f32[1,2,96,256]{3,0,2,1:T(1,128)S(1)} %get-tuple-element.30), channel_id=1, source_target_pairs={{0,1},{1,2},{2,3},{4,5},{5,6},{6,7},{8,9},{9,10},{10,11},{12,13},{... | collective-permute-start | bytes 589832 | tf_op jit(solution)/shard_map/ppermute | solution.py:16
  365.5 9.5 %collective-permute-start.15 = (f32[1,2,96,256]{3,0,2,1:T(1,128)S(1)}, f32[1,2,96,256]{3,0,2,1:T(1,128)S(1)}, u32[]{:S(2)}, u32[]{:S(2)}) collective-permute-start(f32[1,2,96,256]{3,0,2,1:T(1,128)S(1)} %get-tuple-element.31), channel_id=1, source_target_pairs={{1,0},{2,1},{3,2},{5,4},{6,5},{7,6},{9,8},{10,9},{11,10},{13,12},{... | collective-permute-start | bytes 589832 | tf_op jit(solution)/shard_map/ppermute | solution.py:19
  443.1 2.8 copy-start.3
  445.0 0.9 copy-start.7
  447.7 16.1 %copy-start.5 = (f32[2,96,1024]{2,1,0:T(8,128)}, f32[2,96,1024]{2,1,0:T(8,128)S(1)}, u32[]{:S(2)}) copy-start(f32[2,96,1024]{2,1,0:T(8,128)S(1)} %fusion) | copy-start | bytes 2359300
  448.4 9.8 %collective-permute-start.16 = (f32[1,96,256]{2,0,1:T(1,128)S(1)}, f32[1,96,256]{2,0,1:T(1,128)S(1)}, u32[]{:S(2)}, u32[]{:S(2)}) collective-permute-start(f32[1,96,256]{2,0,1:T(1,128)S(1)} %get-tuple-element.20), channel_id=1, source_target_pairs={{0,4},{4,8},{8,12},{12,16},{16,20},{20,24},{24,28},{1,5},{5,9},{9,... | collective-permute-start | bytes 294920 | tf_op jit(solution)/shard_map/ppermute | solution.py:16
  451.0 7.6 %collective-permute-start.17 = (f32[1,96,256]{2,0,1:T(1,128)S(1)}, f32[1,96,256]{2,0,1:T(1,128)S(1)}, u32[]{:S(2)}, u32[]{:S(2)}) collective-permute-start(f32[1,96,256]{2,0,1:T(1,128)S(1)} %get-tuple-element.21), channel_id=1, source_target_pairs={{4,0},{8,4},{12,8},{16,12},{20,16},{24,20},{28,24},{5,1},{9,5},{13... | collective-permute-start | bytes 294920 | tf_op jit(solution)/shard_map/ppermute | solution.py:19
  452.3 9.0 %collective-permute-start.19 = (f32[1,2,96,256]{3,0,2,1:T(1,128)S(1)}, f32[1,2,96,256]{3,0,2,1:T(1,128)S(1)}, u32[]{:S(2)}, u32[]{:S(2)}) collective-permute-start(f32[1,2,96,256]{3,0,2,1:T(1,128)S(1)} %get-tuple-element.25), channel_id=1, source_target_pairs={{1,0},{2,1},{3,2},{5,4},{6,5},{7,6},{9,8},{10,9},{11,10},{13,12},{... | collective-permute-start | bytes 589832 | tf_op jit(solution)/shard_map/ppermute | solution.py:19
  453.6 9.5 %collective-permute-start.18 = (f32[1,2,96,256]{3,0,2,1:T(1,128)S(1)}, f32[1,2,96,256]{3,0,2,1:T(1,128)S(1)}, u32[]{:S(2)}, u32[]{:S(2)}) collective-permute-start(f32[1,2,96,256]{3,0,2,1:T(1,128)S(1)} %get-tuple-element.24), channel_id=1, source_target_pairs={{0,1},{1,2},{2,3},{4,5},{5,6},{6,7},{8,9},{9,10},{10,11},{12,13},{... | collective-permute-start | bytes 589832 | tf_op jit(solution)/shard_map/ppermute | solution.py:16
  530.4 2.2 copy-start.1
  536.9 7.7 %collective-permute-start.20 = (f32[1,96,256]{2,0,1:T(1,128)S(1)}, f32[1,96,256]{2,0,1:T(1,128)S(1)}, u32[]{:S(2)}, u32[]{:S(2)}) collective-permute-start(f32[1,96,256]{2,0,1:T(1,128)S(1)} %get-tuple-element.14), channel_id=1, source_target_pairs={{0,4},{4,8},{8,12},{12,16},{16,20},{20,24},{24,28},{1,5},{5,9},{9,... | collective-permute-start | bytes 294920 | tf_op jit(solution)/shard_map/ppermute | solution.py:16
  538.5 6.5 %collective-permute-start.21 = (f32[1,96,256]{2,0,1:T(1,128)S(1)}, f32[1,96,256]{2,0,1:T(1,128)S(1)}, u32[]{:S(2)}, u32[]{:S(2)}) collective-permute-start(f32[1,96,256]{2,0,1:T(1,128)S(1)} %get-tuple-element.15), channel_id=1, source_target_pairs={{4,0},{8,4},{12,8},{16,12},{20,16},{24,20},{28,24},{5,1},{9,5},{13... | collective-permute-start | bytes 294920 | tf_op jit(solution)/shard_map/ppermute | solution.py:19
  539.8 6.6 %collective-permute-start.22 = (f32[1,2,96,256]{3,0,2,1:T(1,128)S(1)}, f32[1,2,96,256]{3,0,2,1:T(1,128)S(1)}, u32[]{:S(2)}, u32[]{:S(2)}) collective-permute-start(f32[1,2,96,256]{3,0,2,1:T(1,128)S(1)} %get-tuple-element.18), channel_id=1, source_target_pairs={{0,1},{1,2},{2,3},{4,5},{5,6},{6,7},{8,9},{9,10},{10,11},{12,13},{... | collective-permute-start | bytes 589832 | tf_op jit(solution)/shard_map/ppermute | solution.py:16
  543.3 7.6 %collective-permute-start.23 = (f32[1,2,96,256]{3,0,2,1:T(1,128)S(1)}, f32[1,2,96,256]{3,0,2,1:T(1,128)S(1)}, u32[]{:S(2)}, u32[]{:S(2)}) collective-permute-start(f32[1,2,96,256]{3,0,2,1:T(1,128)S(1)} %get-tuple-element.19), channel_id=1, source_target_pairs={{1,0},{2,1},{3,2},{5,4},{6,5},{7,6},{9,8},{10,9},{11,10},{13,12},{... | collective-permute-start | bytes 589832 | tf_op jit(solution)/shard_map/ppermute | solution.py:19
  617.1 13.4 %copy-start.4 = (f32[2,1024,96]{1,2,0:T(8,128)S(1)}, f32[2,1024,96]{1,2,0:T(8,128)}, u32[]{:S(2)}) copy-start(f32[2,1024,96]{1,2,0:T(8,128)} %copy.170) | copy-start | bytes 2359300
  617.1 13.4 %copy-start.14 = (pred[2,1024]{1,0:T(4,128)(4,1)S(1)}, pred[2,1024]{1,0:T(4,128)(4,1)}, u32[]{:S(2)}) copy-start(pred[2,1024]{1,0:T(4,128)(4,1)} %and_bitcast_fusion) | copy-start | bytes 6148
where the time goes:
time: 644 us; the launch traced here: 632 us
  local copies, waits for them, and re-layouts  260 us (40%)
  blocking collectives  241 us (37%)
  starting transfers between devices  49.9 us (8%)
  waiting for transfers between devices  28.5 us (4%)
  other arithmetic  27.6 us (4%)
  matrix products  22.5 us (3%)
    gather x5, local copies, waits for them, and re-layouts, reorder_block(): rows_first = jnp.take(matrix, order, axis=0)  96.7 us
    gather x2, local copies, waits for them, and re-layouts, reorder_block(): both = jnp.take(swapped, order, axis=0)  81.3 us
    psum x2, blocking collectives, shards(): lax.psum(jnp.sum(projected * precond, axis=(0, 2)), ('sub', 'grp'))  78 us
    all_gather x5, blocking collectives, gathered(): grouped = lax.all_gather(coeffs[None], 'grp', axis=0, tiled=True)  66.2 us
    all_gather x5, blocking collectives, gathered(): everything = lax.all_gather(grouped, 'sub', axis=1, tiled=True)  53.9 us
    psum x1, blocking collectives, shards(): curvature = lax.psum(partial_dot, ('sub', 'grp'))  43.3 us
    ppermute x12, starting transfers between devices, extended(): lax.ppermute(lax.slice_in_dim(block, block.shape[dim] - width, None, axis...  34 us
    ppermute x12, waiting for transfers between devices, extended(): lax.ppermute(lax.slice_in_dim(block, 0, width, axis=dim), axis, backward)  20.5 us
  transfers between devices with their start and end apart: 24, of which 10 were waited for; matrix products, arithmetic and copies ran while one was open for 34% of the time, Pallas kernels for 0%

commit v1 on v0

--- a/solution.py
+++ b/solution.py
@@ -6,6 +6,32 @@
 MODES = 6
 ITERS = 2
 HIGHEST = lax.Precision.HIGHEST
+
+
+def recast_the_sides(array_here, k_dim):
+    array_here = jnp.moveaxis(array_here, 0, k_dim)
+    val2 = array_here.shape
+    s_next = array_here.reshape(*val2[:k_dim], val2[k_dim] * val2[k_dim + 1], *val2[k_dim + 2 :])
+    return s_next
+
+
+def define_run_in(point, which_axis, in_dim=0):
+    world_n = lax.axis_size(which_axis)
+    found = list(map(lambda j: (j, (j + 1) % world_n), range(world_n)))
+    entries = [(ii, q) for q, ii in found]
+    now, p_next = ([], [])
+    for src_i in tuple(range(world_n - 1)):
+        if src_i % 2 == 0:
+            now.append(lax.ppermute(now[-1] if now else point, axis_name=which_axis, perm=found))
+        else:
+            p_next.append(
+                lax.ppermute(p_next[-1] if p_next else point, axis_name=which_axis, perm=entries)
+            )
+    found_now = jnp.stack([*now[::-1], point, *p_next], axis=0)
+    state_now = lax.axis_index(which_axis) - len(now)
+    found_now = found_now[(jnp.arange(world_n) - state_now) % world_n]
+    last = recast_the_sides(found_now, in_dim)
+    return last
 
 
 def extended(block, sides, width):
@@ -105,7 +131,7 @@
         return jnp.einsum("skm,snm->skn", weighted_modes, values, precision=HIGHEST)
 
     def gathered(coeffs):
-        grouped = lax.all_gather(coeffs[None], "grp", axis=0, tiled=True)
+        grouped = define_run_in(coeffs[None], "grp")
         everything = lax.all_gather(grouped, "sub", axis=1, tiled=True)
         return everything.reshape(-1, columns)
 

time: 644 us -> 622 us (0.966)
  blocking collectives: 241 us -> 172 us
  starting transfers between devices: 49.9 us -> 74.5 us
  waiting for transfers between devices: 28.5 us -> 40.4 us
    all_gather x5 -> x0, blocking collectives: 66.2 us -> none  [gathered(): grouped = lax.all_gather(coeffs[None], 'grp', axis=0, tiled=True)]
    ppermute x0 -> x15, starting transfers between devices: none -> 22.7 us  [the longest x10 12.2 us: define_run_in(): lax.ppermute(now[-1] if now else point, axis_name=which_axis, perm=found)]
    ppermute x0 -> x15, waiting for transfers between devices: none -> 10.1 us  [the longest x10 10 us: define_run_in(): lax.ppermute(now[-1] if now else point, axis_name=which_axis, perm=found)]
  transfers between devices with their start and end apart: 24 -> 39, of which waited for: 10 -> 15; matrix products, arithmetic and copies ran while one was open for 34% -> 36% of each run, Pallas kernels for 0% -> 0%
where the time goes in v1:
time: 622 us; the launch traced here: 610 us
  local copies, waits for them, and re-layouts  265 us (43%)
  blocking collectives  172 us (28%)
  starting transfers between devices  74.5 us (12%)
  waiting for transfers between devices  40.4 us (6%)
  other arithmetic  32.5 us (5%)
  matrix products  22.4 us (4%)
    gather x5, local copies, waits for them, and re-layouts, reorder_block(): rows_first = jnp.take(matrix, order, axis=0)  96.6 us
    gather x2, local copies, waits for them, and re-layouts, reorder_block(): both = jnp.take(swapped, order, axis=0)  81.4 us
    psum x2, blocking collectives, shards(): lax.psum(jnp.sum(projected * precond, axis=(0, 2)), ('sub', 'grp'))  78.9 us
    all_gather x5, blocking collectives, gathered(): everything = lax.all_gather(grouped, 'sub', axis=1, tiled=True)  52.1 us
    psum x1, blocking collectives, shards(): curvature = lax.psum(partial_dot, ('sub', 'grp'))  41 us
    ppermute x12, starting transfers between devices, extended(): lax.ppermute(lax.slice_in_dim(block, block.shape[dim] - width, None, axis...  36.1 us
    ppermute x12, waiting for transfers between devices, extended(): lax.ppermute(lax.slice_in_dim(block, 0, width, axis=dim), axis, backward)  21.9 us
    ppermute x12, starting transfers between devices, extended(): lax.ppermute(lax.slice_in_dim(block, 0, width, axis=dim), axis, backward)  15.7 us
  transfers between devices with their start and end apart: 39, of which 15 were waited for; matrix products, arithmetic and copies ran while one was open for 36% of the time, Pallas kernels for 0%

profile of v1, /device:TPU:0, one launch (start us, length us, event | category | flops | bytes accessed | tf_op | source)
XLA Modules:
  0.0 609.5 jit_solution(8832483640341701977)
XLA Ops:
  2.7 1.5 copy.54
  4.1 13.0 %gather_fusion.6 = f32[2048,96]{1,0:T(8,128)S(1)} fusion(f32[2,96,1024]{1,2,0:T(8,128)S(1)} %bitcast.410, s32[2048]{0:T(1024)S(1)} %bitcast.409), kind=kCustom, calls=%fused_computation.clone | custom fusion | bytes 1589248 | tf_op jit(solution)/shard_map/jit(take_along_axis)/gather | solution.py:88
  19.0 2.4 collective-permute-start
  23.7 5.0 collective-permute-start.2
  30.4 13.0 %gather_fusion.5 = f32[2048,6]{1,0:T(8,128)S(1)} fusion(f32[2,6,1024]{1,2,0:T(8,128)S(1)} %bitcast.425, s32[2048]{0:T(1024)S(1)} %get-tuple-element.61), kind=kCustom, calls=%fused_computation.12 | custom fusion | bytes 114688 | tf_op jit(solution)/shard_map/jit(take_along_axis)/gather | solution.py:106
  44.0 4.0 collective-permute-start.7
  49.1 42.1 %gather_fusion.7 = bf16[2048,1024]{1,0:T(8,128)(2,1)} fusion(bf16[2,1024,1024]{2,1,0:T(8,128)(2,1)} %bitcast.407, s32[2048]{0:T(1024)S(1)} %get-tuple-element.60), kind=kCustom, calls=%fused_computation.1.clone | custom fusion | bytes 8404992 | tf_op jit(solution)/shard_map/vmap(jit(_take))/gather | solution.py:60
  91.2 6.2 %copy.80 = bf16[2,1024,1024]{1,2,0:T(8,128)(2,1)} copy(bf16[2,1024,1024]{2,1,0:T(8,128)(2,1)} %bitcast.411) | data formatting | bytes 8388608 | tf_op jit(solution)/shard_map/vmap(jit(_take))/gather | solution.py:60
  97.4 42.1 %gather_fusion.9 = bf16[2048,1024]{1,0:T(8,128)(2,1)} fusion(bf16[2,1024,1024]{2,1,0:T(8,128)(2,1)} %bitcast.408, s32[2048]{0:T(1024)S(1)} %get-tuple-element.60), kind=kCustom, calls=%fused_computation.5.clone | custom fusion | bytes 8404992 | tf_op jit(solution)/shard_map/vmap(jit(_take))/gather | solution.py:60
  139.4 6.2 %copy.88 = bf16[2,1024,1024]{1,2,0:T(8,128)(2,1)} copy(bf16[2,1024,1024]{2,1,0:T(8,128)(2,1)} %bitcast.412) | data formatting | bytes 8388608 | tf_op jit(solution)/shard_map/vmap(jit(_take))/gather | solution.py:60
  147.0 3.3 collective-permute-done.8
  150.3 5.2 collective-permute-start.9
  159.1 1.7 pad_maximum_fusion
  162.1 2.7 collective-permute-start.4
  165.6 2.1 collective-permute-start.6
  169.3 4.5 collective-permute-done.5
  174.4 12.2 %all-gather = f32[4,16,6,96]{3,2,1,0:T(8,128)S(1)} all-gather(f32[4,2,6,96]{3,2,1,0:T(8,128)S(1)} %gather_fusion), channel_id=2, replica_groups=mesh['sub'=8,'grp'=4] {'sub'}, dimensions={1}, use_global_device_ids=true | all-gather | bytes 165888 | tf_op jit(solution)/shard_map/all_gather | solution.py:135
  190.0 6.1 %select_bitcast_fusion = (bf16[2,1024,1024]{2,1,0:T(8,128)(2,1)}, bf16[2,1024,1024]{2,1,0:T(8,128)(2,1)}) fusion(bf16[2,1024,1024]{1,2,0:T(8,128)(2,1)} %copy.88, pred[2,1024]{1,0:T(4,128)(4,1)S(1)} %copy-done.17, bf16[2,1024,1024]{1,2,0:T(8,128)(2,1)S(1)} %copy-done), kind=kLoop, calls=%fused_computation.14 | loop fusion | flops 4194304 | bytes 16779264 | tf_op jit(solution)/shard_map/vmap()/transpose | solution.py:61
  196.1 3.8 collective-permute-start.13
  200.6 40.8 %gather_fusion.8 = bf16[2048,1024]{1,0:T(8,128)(2,1)} fusion(bf16[2,1024,1024]{2,1,0:T(8,128)(2,1)} %get-tuple-element.57, s32[2048]{0:T(1024)S(1)} %get-tuple-element.60), kind=kCustom, calls=%fused_computation.4.clone | custom fusion | bytes 8404992 | tf_op jit(solution)/shard_map/vmap(jit(_take))/gather | solution.py:62
  242.1 7.9 %all-gather.1 = f32[4,16,6,96]{3,2,1,0:T(8,128)S(1)} all-gather(f32[4,2,6,96]{3,2,1,0:T(8,128)S(1)} %gather_fusion.1), channel_id=3, replica_groups=mesh['sub'=8,'grp'=4] {'sub'}, dimensions={1}, use_global_device_ids=true | all-gather | bytes 165888 | tf_op jit(solution)/shard_map/all_gather | solution.py:135
  252.8 1.7 fusion.1
  255.2 2.3 collective-permute-start.14
  260.4 1.5 collective-permute-start.17
  264.0 4.7 collective-permute-done.17
  269.8 2.0 multiply_reduce_fusion.3
  272.6 4.0 collective-permute-start.18
  277.5 1.5 collective-permute-done.18
  280.9 40.7 %gather_fusion.10 = bf16[2048,1024]{1,0:T(8,128)(2,1)} fusion(bf16[2,1024,1024]{2,1,0:T(8,128)(2,1)} %get-tuple-element.56, s32[2048]{0:T(1024)S(1)} %get-tuple-element.60), kind=kCustom, calls=%fused_computation.6.clone | custom fusion | bytes 8404992 | tf_op jit(solution)/shard_map/vmap(jit(_take))/gather | solution.py:62
  322.2 11.6 %all-gather.2 = f32[4,16,6,96]{3,2,1,0:T(8,128)S(1)} all-gather(f32[4,2,6,96]{3,2,1,0:T(8,128)S(1)} %gather_fusion.2), channel_id=4, replica_groups=mesh['sub'=8,'grp'=4] {'sub'}, dimensions={1}, use_global_device_ids=true | all-gather | bytes 165888 | tf_op jit(solution)/shard_map/all_gather | solution.py:135
  336.7 1.7 fusion.3
  339.1 2.3 collective-permute-start.21
  343.0 3.9 collective-permute-start.23
  349.0 3.0 collective-permute-done.23
  352.0 4.4 collective-permute-done.24
  359.9 38.4 %all-reduce = (f32[96]{0:T(128)S(1)}, f32[96]{0:T(128)S(1)}) all-reduce(f32[96]{0:T(128)S(1)} %copy-done.25, f32[96]{0:T(128)S(1)} %get-tuple-element.10), channel_id=1, replica_groups=mesh['sub'=8,'grp'=4] {'sub','grp'}, use_global_device_ids=true, to_apply=%region_1.4 | all-reduce | flops 192 | bytes 1536 | tf_op jit(solution)/shard_map/psum | solution.py:160
  399.8 1.8 collective-permute-start.25
  401.6 2.1 collective-permute-start.27
  403.6 1.7 collective-permute-done.25
  405.3 8.0 %scatter_custom_fusion = s32[2048]{0:T(1024)S(1)} fusion(s32[2048]{0:T(1024)S(1)} %get-tuple-element.65, s32[2048]{0:T(1024)S(1)} %get-tuple-element.64, s32[]{:T(128)} %constant.75.clone.1), kind=kCustom, calls=%fused_computation.195 | custom fusion | bytes 8196
  414.1 10.1 %all-gather.3 = f32[4,16,6,96]{3,2,1,0:T(8,128)S(1)} all-gather(f32[4,2,6,96]{3,2,1,0:T(8,128)S(1)} %gather_fusion.3), channel_id=5, replica_groups=mesh['sub'=8,'grp'=4] {'sub'}, dimensions={1}, use_global_device_ids=true | all-gather | bytes 165888 | tf_op jit(solution)/shard_map/all_gather | solution.py:135
  427.6 1.7 fusion
  430.0 2.2 collective-permute-start.28
  433.9 2.5 collective-permute-start.30
  438.5 2.4 collective-permute-done.30
  441.0 4.7 collective-permute-done.31
  447.8 1.9 multiply_reduce_fusion.1
  450.4 2.1 collective-permute-start.32
  452.5 1.8 collective-permute-start.34
  454.3 1.6 collective-permute-done.32
  456.3 40.5 %psum.30 = f32[96]{0:T(128)S(1)} all-reduce(f32[96]{0:T(128)S(1)} %get-tuple-element.8), channel_id=1, replica_groups=mesh['sub'=8,'grp'=4] {'sub','grp'}, use_global_device_ids=true, to_apply=%region_5.8 | all-reduce | flops 96 | bytes 768 | tf_op jit(solution)/shard_map/psum | solution.py:160
  497.9 10.3 %all-gather.4 = f32[4,16,6,96]{3,2,1,0:T(8,128)S(1)} all-gather(f32[4,2,6,96]{3,2,1,0:T(8,128)S(1)} %gather_fusion.4), channel_id=6, replica_groups=mesh['sub'=8,'grp'=4] {'sub'}, dimensions={1}, use_global_device_ids=true | all-gather | bytes 165888 | tf_op jit(solution)/shard_map/all_gather | solution.py:135
  511.0 2.5 fusion.2
  513.4 1.5 reshape.280
  515.3 2.3 collective-permute-start.35
  519.2 2.9 collective-permute-start.37
  524.3 1.7 collective-permute-done.37
  526.0 4.7 collective-permute-done.38
  532.7 2.5 multiply_reduce_fusion
  535.2 41.0 %psum.31 = f32[96]{0:T(128)S(1)} all-reduce(f32[96]{0:T(128)S(1)} %get-tuple-element.6), channel_id=1, replica_groups=mesh['sub'=8,'grp'=4] {'sub','grp'}, use_global_device_ids=true, to_apply=%region_7.10 | all-reduce | flops 96 | bytes 768 | tf_op jit(solution)/shard_map/psum | solution.py:167
  576.3 2.3 multiply_subtract_fusion
  578.6 1.5 copy.107
  580.0 13.0 %gather_fusion.11 = f32[2048,96]{1,0:T(8,128)S(1)} fusion(f32[2,96,1024]{1,2,0:T(8,128)S(1)} %copy.107, s32[2048]{0:T(1024)S(1)} %bitcast.405), kind=kCustom, calls=%fused_computation.2.clone | custom fusion | bytes 1589248 | tf_op jit(solution)/shard_map/jit(take_along_axis)/gather | solution.py:172
  594.7 13.0 %gather_fusion.12 = f32[2048,96]{1,0:T(8,128)S(1)} fusion(f32[2,96,1024]{1,2,0:T(8,128)S(1)} %copy.109, s32[2048]{0:T(1024)S(1)} %bitcast.406), kind=kCustom, calls=%fused_computation.3.clone | custom fusion | bytes 1589248 | tf_op jit(solution)/shard_map/jit(take_along_axis)/gather | solution.py:173
  (260 shorter events, 73.4 us)
Async XLA Ops:
  17.2 12.8 %copy-start.15 = (f32[1,2,6,1024]{3,1,2,0:T(2,128)S(1)}, f32[1,2,6,1024]{3,1,2,0:T(2,128)}, u32[]{:S(2)}) copy-start(f32[1,2,6,1024]{3,1,2,0:T(2,128)} %param.13) | copy-start | bytes 147460
  17.5 26.3 %copy-start.10 = (s32[1,2,1024]{2,1,0:T(2,128)S(1)}, s32[1,2,1024]{2,1,0:T(2,128)}, u32[]{:S(2)}) copy-start(s32[1,2,1024]{2,1,0:T(2,128)} %param.15) | copy-start | bytes 24580
  17.5 26.3 %copy-start.14 = (f32[1,2,6,384]{3,1,2,0:T(2,128)S(1)}, f32[1,2,6,384]{3,1,2,0:T(2,128)}, u32[]{:S(2)}) copy-start(f32[1,2,6,384]{3,1,2,0:T(2,128)} %param.14) | copy-start | bytes 55300
  19.0 137.1 %collective-permute-start = (f32[1,96,256]{2,0,1:T(1,128)S(1)}, f32[1,96,256]{2,0,1:T(1,128)S(1)}, u32[]{:S(2)}, u32[]{:S(2)}) collective-permute-start(f32[1,96,256]{2,0,1:T(1,128)S(1)} %get-tuple-element.38), channel_id=1, source_target_pairs={{0,4},{4,8},{8,12},{12,16},{16,20},{20,24},{24,28},{1,5},{5,9},{9,... | collective-permute-start | bytes 294920 | tf_op jit(solution)/shard_map/ppermute | solution.py:42
  21.3 136.4 %collective-permute-start.1 = (f32[1,96,256]{2,0,1:T(1,128)}, f32[1,96,256]{2,0,1:T(1,128)}, u32[]{:S(2)}, u32[]{:S(2)}) collective-permute-start(f32[1,96,256]{2,0,1:T(1,128)} %get-tuple-element.39), channel_id=1, source_target_pairs={{4,0},{8,4},{12,8},{16,12},{20,16},{24,20},{28,24},{5,1},{9,5},{13... | collective-permute-start | bytes 294920 | tf_op jit(solution)/shard_map/ppermute | solution.py:45
  23.7 135.3 %collective-permute-start.2 = (f32[1,2,96,256]{3,0,2,1:T(1,128)}, f32[1,2,96,256]{3,0,2,1:T(1,128)}, u32[]{:S(2)}, u32[]{:S(2)}) collective-permute-start(f32[1,2,96,256]{3,0,2,1:T(1,128)} %get-tuple-element.42), channel_id=1, source_target_pairs={{0,1},{1,2},{2,3},{4,5},{5,6},{6,7},{8,9},{9,10},{10,11},{12,13},{... | collective-permute-start | bytes 589832 | tf_op jit(solution)/shard_map/ppermute | solution.py:42
  28.7 130.4 %collective-permute-start.3 = (f32[1,2,96,256]{3,0,2,1:T(1,128)}, f32[1,2,96,256]{3,0,2,1:T(1,128)}, u32[]{:S(2)}, u32[]{:S(2)}) collective-permute-start(f32[1,2,96,256]{3,0,2,1:T(1,128)} %get-tuple-element.43), channel_id=1, source_target_pairs={{1,0},{2,1},{3,2},{5,4},{6,5},{7,6},{9,8},{10,9},{11,10},{13,12},{... | collective-permute-start | bytes 589832 | tf_op jit(solution)/shard_map/ppermute | solution.py:45
  44.0 101.7 %collective-permute-start.7 = (f32[1,6,640]{2,1,0:T(8,128)S(1)}, f32[1,6,640]{2,1,0:T(8,128)S(1)}, u32[]{:S(2)}, u32[]{:S(2)}) collective-permute-start(f32[1,6,640]{2,1,0:T(8,128)S(1)} %get-tuple-element.44), channel_id=1, source_target_pairs={{0,4},{4,8},{8,12},{12,16},{16,20},{20,24},{24,28},{1,5},{5,9},{9,... | collective-permute-start | bytes 46088 | tf_op jit(solution)/shard_map/ppermute | solution.py:42
  48.0 43.1 %copy-start.16 = (pred[2,1024]{1,0:T(4,128)(4,1)}, pred[2,1024]{1,0:T(4,128)(4,1)S(1)}, u32[]{:S(2)}) copy-start(pred[2,1024]{1,0:T(4,128)(4,1)S(1)} %compare_and_fusion.1) | copy-start | bytes 6148
  49.0 124.8 %copy-start.20 = (s32[1024]{0:T(1024)}, s32[1024]{0:T(1024)S(1)}, u32[]{:S(2)}) copy-start(s32[1024]{0:T(1024)S(1)} %pad_clamp_fusion) | copy-start | bytes 12292
  145.7 4.6 collective-permute-start.8
  150.3 14.5 %collective-permute-start.9 = (f32[1,2,6,640]{3,2,1,0:T(8,128)}, f32[1,2,6,640]{3,2,1,0:T(8,128)}, u32[]{:S(2)}, u32[]{:S(2)}) collective-permute-start(f32[1,2,6,640]{3,2,1,0:T(8,128)} %get-tuple-element.48), channel_id=1, source_target_pairs={{0,1},{1,2},{2,3},{4,5},{5,6},{6,7},{8,9},{9,10},{10,11},{12,13},{... | collective-permute-start | bytes 92168 | tf_op jit(solution)/shard_map/ppermute | solution.py:42
  156.1 8.7 %collective-permute-start.10 = (f32[1,2,6,640]{3,2,1,0:T(8,128)}, f32[1,2,6,640]{3,2,1,0:T(8,128)}, u32[]{:S(2)}, u32[]{:S(2)}) collective-permute-start(f32[1,2,6,640]{3,2,1,0:T(8,128)} %get-tuple-element.49), channel_id=1, source_target_pairs={{1,0},{2,1},{3,2},{5,4},{6,5},{7,6},{9,8},{10,9},{11,10},{13,12},{... | collective-permute-start | bytes 92168 | tf_op jit(solution)/shard_map/ppermute | solution.py:45
  160.8 4.0 copy-start.9
  162.1 6.3 %collective-permute-start.4 = (f32[1,2,6,96]{3,2,1,0:T(8,128)S(1)}, f32[1,2,6,96]{3,2,1,0:T(8,128)S(1)}, u32[]{:S(2)}, u32[]{:S(2)}) collective-permute-start(f32[1,2,6,96]{3,2,1,0:T(8,128)S(1)} %bitcast.438), channel_id=1, source_target_pairs={{0,1},{1,2},{2,3},{3,0},{4,5},{5,6},{6,7},{7,4},{8,9},{9,10},{10,1... | collective-permute-start | bytes 13832 | tf_op jit(solution)/shard_map/ppermute | solution.py:25
  165.6 3.7 collective-permute-start.6
  168.4 5.4 collective-permute-start.5
  186.7 3.3 copy-start.17
  187.0 3.0 copy-start
  189.9 10.0 %copy-start.11 = (s32[2,1024,1]{1,0,2:T(2,128)S(1)}, s32[2,1024,1]{1,0,2:T(2,128)}, u32[]{:S(2)}) copy-start(s32[2,1024,1]{1,0,2:T(2,128)} %get-tuple-element.50) | copy-start | bytes 24580
  189.9 10.0 %copy-start.24 = (s32[2]{0:T(128)S(1)}, s32[2]{0:T(128)}, u32[]{:S(2)}) copy-start(s32[2]{0:T(128)} %constant.99) | copy-start | bytes 28
  189.9 10.0 %collective-permute-start.11 = (f32[1,2,6,96]{3,2,1,0:T(8,128)S(1)}, f32[1,2,6,96]{3,2,1,0:T(8,128)S(1)}, u32[]{:S(2)}, u32[]{:S(2)}) collective-permute-start(f32[1,2,6,96]{3,2,1,0:T(8,128)S(1)} %bitcast.444), channel_id=1, source_target_pairs={{0,1},{1,2},{2,3},{3,0},{4,5},{5,6},{6,7},{7,4},{8,9},{9,10},{10,1... | collective-permute-start | bytes 13832 | tf_op jit(solution)/shard_map/ppermute | solution.py:25
  196.1 45.3 %collective-permute-start.13 = (f32[1,2,6,96]{3,2,1,0:T(8,128)S(1)}, f32[1,2,6,96]{3,2,1,0:T(8,128)S(1)}, u32[]{:S(2)}, u32[]{:S(2)}) collective-permute-start(f32[1,2,6,96]{3,2,1,0:T(8,128)S(1)} %bitcast.445), channel_id=1, source_target_pairs={{1,0},{2,1},{3,2},{0,3},{5,4},{6,5},{7,6},{4,7},{9,8},{10,9},{11,1... | collective-permute-start | bytes 13832 | tf_op jit(solution)/shard_map/ppermute | solution.py:28
  199.9 41.5 %collective-permute-start.12 = (f32[1,2,6,96]{3,2,1,0:T(8,128)S(1)}, f32[1,2,6,96]{3,2,1,0:T(8,128)S(1)}, u32[]{:S(2)}, u32[]{:S(2)}) collective-permute-start(f32[1,2,6,96]{3,2,1,0:T(8,128)S(1)} %collective-permute-done.11), channel_id=1, source_target_pairs={{0,1},{1,2},{2,3},{3,0},{4,5},{5,6},{6,7},{7,4},{8,9},{9,10},{10,1... | collective-permute-start | bytes 13832 | tf_op jit(solution)/shard_map/ppermute | solution.py:25
  199.9 41.4 %copy-start.12 = (s32[2,1024,1]{1,0,2:T(2,128)}, s32[2,1024,1]{1,0,2:T(2,128)S(1)}, u32[]{:S(2)}) copy-start(s32[2,1024,1]{1,0,2:T(2,128)S(1)} %iota.19) | copy-start | bytes 24580
  250.6 2.2 copy-start.3
  252.5 2.4 copy-start.8
  255.2 6.7 %collective-permute-start.14 = (f32[1,96,256]{2,0,1:T(1,128)S(1)}, f32[1,96,256]{2,0,1:T(1,128)S(1)}, u32[]{:S(2)}, u32[]{:S(2)}) collective-permute-start(f32[1,96,256]{2,0,1:T(1,128)S(1)} %get-tuple-element.32), channel_id=1, source_target_pairs={{0,4},{4,8},{8,12},{12,16},{16,20},{20,24},{24,28},{1,5},{5,9},{9,... | collective-permute-start | bytes 294920 | tf_op jit(solution)/shard_map/ppermute | solution.py:42
  257.8 4.6 collective-permute-start.15
  259.1 4.9 collective-permute-start.16
  260.4 8.2 %collective-permute-start.17 = (f32[1,2,96,256]{3,0,2,1:T(1,128)S(1)}, f32[1,2,96,256]{3,0,2,1:T(1,128)S(1)}, u32[]{:S(2)}, u32[]{:S(2)}) collective-permute-start(f32[1,2,96,256]{3,0,2,1:T(1,128)S(1)} %get-tuple-element.37), channel_id=1, source_target_pairs={{1,0},{2,1},{3,2},{5,4},{6,5},{7,6},{9,8},{10,9},{11,10},{13,12},{... | collective-permute-start | bytes 589832 | tf_op jit(solution)/shard_map/ppermute | solution.py:45
  262.2 14.4 %copy-start.13 = (s32[2,1024,1]{1,0,2:T(2,128)S(1)}, s32[2,1024,1]{1,0,2:T(2,128)}, u32[]{:S(2)}) copy-start(s32[2,1024,1]{1,0,2:T(2,128)} %copy-done.12) | copy-start | bytes 24580
  262.2 14.4 %copy-start.23 = (s32[2]{0:T(128)S(1)}, s32[2]{0:T(128)}, u32[]{:S(2)}) copy-start(s32[2]{0:T(128)} %constant.96) | copy-start | bytes 28
  262.2 18.1 %copy-start.19 = (pred[2,1024]{1,0:T(4,128)(4,1)S(1)}, pred[2,1024]{1,0:T(4,128)(4,1)}, u32[]{:S(2)}) copy-start(pred[2,1024]{1,0:T(4,128)(4,1)} %and_reduce_fusion) | copy-start | bytes 6148
  272.6 6.3 %collective-permute-start.18 = (f32[1,2,6,96]{3,2,1,0:T(8,128)S(1)}, f32[1,2,6,96]{3,2,1,0:T(8,128)S(1)}, u32[]{:S(2)}, u32[]{:S(2)}) collective-permute-start(f32[1,2,6,96]{3,2,1,0:T(8,128)S(1)} %bitcast.447), channel_id=1, source_target_pairs={{0,1},{1,2},{2,3},{3,0},{4,5},{5,6},{6,7},{7,4},{8,9},{9,10},{10,1... | collective-permute-start | bytes 13832 | tf_op jit(solution)/shard_map/ppermute | solution.py:25
  276.6 44.9 %collective-permute-start.20 = (f32[1,2,6,96]{3,2,1,0:T(8,128)S(1)}, f32[1,2,6,96]{3,2,1,0:T(8,128)S(1)}, u32[]{:S(2)}, u32[]{:S(2)}) collective-permute-start(f32[1,2,6,96]{3,2,1,0:T(8,128)S(1)} %bitcast.448), channel_id=1, source_target_pairs={{1,0},{2,1},{3,2},{0,3},{5,4},{6,5},{7,6},{4,7},{9,8},{10,9},{11,1... | collective-permute-start | bytes 13832 | tf_op jit(solution)/shard_map/ppermute | solution.py:28
  278.9 42.6 %collective-permute-start.19 = (f32[1,2,6,96]{3,2,1,0:T(8,128)S(1)}, f32[1,2,6,96]{3,2,1,0:T(8,128)S(1)}, u32[]{:S(2)}, u32[]{:S(2)}) collective-permute-start(f32[1,2,6,96]{3,2,1,0:T(8,128)S(1)} %collective-permute-done.18), channel_id=1, source_target_pairs={{0,1},{1,2},{2,3},{3,0},{4,5},{5,6},{6,7},{7,4},{8,9},{9,10},{10,1... | collective-permute-start | bytes 13832 | tf_op jit(solution)/shard_map/ppermute | solution.py:25
  334.5 2.2 copy-start.1
  339.1 20.8 %copy-start.25 = (f32[96]{0:T(128)S(1)}, f32[96]{0:T(128)}, u32[]{:S(2)}) copy-start(f32[96]{0:T(128)} %get-tuple-element.12) | copy-start | bytes 1156
  339.1 9.1 %collective-permute-start.21 = (f32[1,96,256]{2,0,1:T(1,128)S(1)}, f32[1,96,256]{2,0,1:T(1,128)S(1)}, u32[]{:S(2)}, u32[]{:S(2)}) collective-permute-start(f32[1,96,256]{2,0,1:T(1,128)S(1)} %get-tuple-element.26), channel_id=1, source_target_pairs={{0,4},{4,8},{8,12},{12,16},{16,20},{20,24},{24,28},{1,5},{5,9},{9,... | collective-permute-start | bytes 294920 | tf_op jit(solution)/shard_map/ppermute | solution.py:42
  341.7 6.9 %collective-permute-start.22 = (f32[1,96,256]{2,0,1:T(1,128)S(1)}, f32[1,96,256]{2,0,1:T(1,128)S(1)}, u32[]{:S(2)}, u32[]{:S(2)}) collective-permute-start(f32[1,96,256]{2,0,1:T(1,128)S(1)} %get-tuple-element.27), channel_id=1, source_target_pairs={{4,0},{8,4},{12,8},{16,12},{20,16},{24,20},{28,24},{5,1},{9,5},{13... | collective-permute-start | bytes 294920 | tf_op jit(solution)/shard_map/ppermute | solution.py:45
  343.0 9.0 %collective-permute-start.23 = (f32[1,2,96,256]{3,0,2,1:T(1,128)S(1)}, f32[1,2,96,256]{3,0,2,1:T(1,128)S(1)}, u32[]{:S(2)}, u32[]{:S(2)}) collective-permute-start(f32[1,2,96,256]{3,0,2,1:T(1,128)S(1)} %get-tuple-element.30), channel_id=1, source_target_pairs={{0,1},{1,2},{2,3},{4,5},{5,6},{6,7},{8,9},{9,10},{10,11},{12,13},{... | collective-permute-start | bytes 589832 | tf_op jit(solution)/shard_map/ppermute | solution.py:42
  346.9 9.5 %collective-permute-start.24 = (f32[1,2,96,256]{3,0,2,1:T(1,128)S(1)}, f32[1,2,96,256]{3,0,2,1:T(1,128)S(1)}, u32[]{:S(2)}, u32[]{:S(2)}) collective-permute-start(f32[1,2,96,256]{3,0,2,1:T(1,128)S(1)} %get-tuple-element.31), channel_id=1, source_target_pairs={{1,0},{2,1},{3,2},{5,4},{6,5},{7,6},{9,8},{10,9},{11,10},{13,12},{... | collective-permute-start | bytes 589832 | tf_op jit(solution)/shard_map/ppermute | solution.py:45
  357.1 48.2 %copy-start.18 = (s32[1,8,2,128]{3,2,1,0:T(2,128)S(1)}, s32[1,8,2,128]{3,2,1,0:T(2,128)}, u32[]{:S(2)}) copy-start(s32[1,8,2,128]{3,2,1,0:T(2,128)} %select_bitcast_fusion.5) | copy-start | bytes 24580
  399.8 5.5 collective-permute-start.25
  401.6 11.8 %collective-permute-start.27 = (f32[1,2,6,96]{3,2,1,0:T(8,128)S(1)}, f32[1,2,6,96]{3,2,1,0:T(8,128)S(1)}, u32[]{:S(2)}, u32[]{:S(2)}) collective-permute-start(f32[1,2,6,96]{3,2,1,0:T(8,128)S(1)} %bitcast.442), channel_id=1, source_target_pairs={{1,0},{2,1},{3,2},{0,3},{5,4},{6,5},{7,6},{4,7},{9,8},{10,9},{11,1... | collective-permute-start | bytes 13832 | tf_op jit(solution)/shard_map/ppermute | solution.py:28
  405.3 8.1 %collective-permute-start.26 = (f32[1,2,6,96]{3,2,1,0:T(8,128)S(1)}, f32[1,2,6,96]{3,2,1,0:T(8,128)S(1)}, u32[]{:S(2)}, u32[]{:S(2)}) collective-permute-start(f32[1,2,6,96]{3,2,1,0:T(8,128)S(1)} %collective-permute-done.25), channel_id=1, source_target_pairs={{0,1},{1,2},{2,3},{3,0},{4,5},{5,6},{6,7},{7,4},{8,9},{9,10},{10,1... | collective-permute-start | bytes 13832 | tf_op jit(solution)/shard_map/ppermute | solution.py:25
  424.8 2.8 copy-start.4
  429.3 17.1 %copy-start.6 = (f32[2,96,1024]{2,1,0:T(8,128)}, f32[2,96,1024]{2,1,0:T(8,128)S(1)}, u32[]{:S(2)}) copy-start(f32[2,96,1024]{2,1,0:T(8,128)S(1)} %fusion) | copy-start | bytes 2359300
  430.0 7.7 %collective-permute-start.28 = (f32[1,96,256]{2,0,1:T(1,128)S(1)}, f32[1,96,256]{2,0,1:T(1,128)S(1)}, u32[]{:S(2)}, u32[]{:S(2)}) collective-permute-start(f32[1,96,256]{2,0,1:T(1,128)S(1)} %get-tuple-element.20), channel_id=1, source_target_pairs={{0,4},{4,8},{8,12},{12,16},{16,20},{20,24},{24,28},{1,5},{5,9},{9,... | collective-permute-start | bytes 294920 | tf_op jit(solution)/shard_map/ppermute | solution.py:42
  432.6 5.5 collective-permute-start.29
  433.9 7.0 %collective-permute-start.30 = (f32[1,2,96,256]{3,0,2,1:T(1,128)S(1)}, f32[1,2,96,256]{3,0,2,1:T(1,128)S(1)}, u32[]{:S(2)}, u32[]{:S(2)}) collective-permute-start(f32[1,2,96,256]{3,0,2,1:T(1,128)S(1)} %get-tuple-element.24), channel_id=1, source_target_pairs={{0,1},{1,2},{2,3},{4,5},{5,6},{6,7},{8,9},{9,10},{10,11},{12,13},{... | collective-permute-start | bytes 589832 | tf_op jit(solution)/shard_map/ppermute | solution.py:42
  436.4 9.3 %collective-permute-start.31 = (f32[1,2,96,256]{3,0,2,1:T(1,128)S(1)}, f32[1,2,96,256]{3,0,2,1:T(1,128)S(1)}, u32[]{:S(2)}, u32[]{:S(2)}) collective-permute-start(f32[1,2,96,256]{3,0,2,1:T(1,128)S(1)} %get-tuple-element.25), channel_id=1, source_target_pairs={{1,0},{2,1},{3,2},{5,4},{6,5},{7,6},{9,8},{10,9},{11,10},{13,12},{... | collective-permute-start | bytes 589832 | tf_op jit(solution)/shard_map/ppermute | solution.py:45
  437.9 58.8 %copy-start.27 = (f32[96]{0:T(128)S(1)}, f32[96]{0:T(128)}, u32[]{:S(2)}) copy-start(f32[96]{0:T(128)} %copy-done.26) | copy-start | bytes 1156
  450.4 5.5 collective-permute-start.32
  452.5 44.2 %collective-permute-start.34 = (f32[1,2,6,96]{3,2,1,0:T(8,128)S(1)}, f32[1,2,6,96]{3,2,1,0:T(8,128)S(1)}, u32[]{:S(2)}, u32[]{:S(2)}) collective-permute-start(f32[1,2,6,96]{3,2,1,0:T(8,128)S(1)} %bitcast.451), channel_id=1, source_target_pairs={{1,0},{2,1},{3,2},{0,3},{5,4},{6,5},{7,6},{4,7},{9,8},{10,9},{11,1... | collective-permute-start | bytes 13832 | tf_op jit(solution)/shard_map/ppermute | solution.py:28
  455.9 40.9 %collective-permute-start.33 = (f32[1,2,6,96]{3,2,1,0:T(8,128)S(1)}, f32[1,2,6,96]{3,2,1,0:T(8,128)S(1)}, u32[]{:S(2)}, u32[]{:S(2)}) collective-permute-start(f32[1,2,6,96]{3,2,1,0:T(8,128)S(1)} %collective-permute-done.32), channel_id=1, source_target_pairs={{0,1},{1,2},{2,3},{3,0},{4,5},{5,6},{6,7},{7,4},{8,9},{9,10},{10,1... | collective-permute-start | bytes 13832 | tf_op jit(solution)/shard_map/ppermute | solution.py:25
  515.3 61.0 %copy-start.29 = (f32[96]{0:T(128)S(1)}, f32[96]{0:T(128)}, u32[]{:S(2)}) copy-start(f32[96]{0:T(128)} %copy-done.28) | copy-start | bytes 1156
  515.3 61.0 %copy-start.22 = (f32[96]{0:T(128)S(1)}, f32[96]{0:T(128)}, u32[]{:S(2)}) copy-start(f32[96]{0:T(128)} %copy-done.21) | copy-start | bytes 1156
  515.3 8.2 %collective-permute-start.35 = (f32[1,96,256]{2,0,1:T(1,128)S(1)}, f32[1,96,256]{2,0,1:T(1,128)S(1)}, u32[]{:S(2)}, u32[]{:S(2)}) collective-permute-start(f32[1,96,256]{2,0,1:T(1,128)S(1)} %get-tuple-element.14), channel_id=1, source_target_pairs={{0,4},{4,8},{8,12},{12,16},{16,20},{20,24},{24,28},{1,5},{5,9},{9,... | collective-permute-start | bytes 294920 | tf_op jit(solution)/shard_map/ppermute | solution.py:42
  517.9 6.0 collective-permute-start.36
  519.2 6.8 %collective-permute-start.37 = (f32[1,2,96,256]{3,0,2,1:T(1,128)S(1)}, f32[1,2,96,256]{3,0,2,1:T(1,128)S(1)}, u32[]{:S(2)}, u32[]{:S(2)}) collective-permute-start(f32[1,2,96,256]{3,0,2,1:T(1,128)S(1)} %get-tuple-element.18), channel_id=1, source_target_pairs={{0,1},{1,2},{2,3},{4,5},{5,6},{6,7},{8,9},{9,10},{10,11},{12,13},{... | collective-permute-start | bytes 589832 | tf_op jit(solution)/shard_map/ppermute | solution.py:42
  522.1 8.6 %collective-permute-start.38 = (f32[1,2,96,256]{3,0,2,1:T(1,128)S(1)}, f32[1,2,96,256]{3,0,2,1:T(1,128)S(1)}, u32[]{:S(2)}, u32[]{:S(2)}) collective-permute-start(f32[1,2,96,256]{3,0,2,1:T(1,128)S(1)} %get-tuple-element.19), channel_id=1, source_target_pairs={{1,0},{2,1},{3,2},{5,4},{6,5},{7,6},{9,8},{10,9},{11,10},{13,12},{... | collective-permute-start | bytes 589832 | tf_op jit(solution)/shard_map/ppermute | solution.py:45
  594.6 13.4 %copy-start.5 = (f32[2,1024,96]{1,2,0:T(8,128)S(1)}, f32[2,1024,96]{1,2,0:T(8,128)}, u32[]{:S(2)}) copy-start(f32[2,1024,96]{1,2,0:T(8,128)} %copy.108) | copy-start | bytes 2359300
  (5 other events, 4.7 us)
